TPU v7x, 32 devices: a whole 2x2x4 slice. The times are simulated.
32 devices in a mesh: groups: 2 (over y), ctx: 4 (over z), fsdp: 2 (over x), sub: 2 (over core).
Axes of the slice: x: 2, y: 2, z: 4, core: 2. Of those that a mesh axis runs over, the one named last changes fastest.
Arguments:
- layer_input: bfloat16 [4, 2048, 2304], P(('groups', 'fsdp'), ('ctx', 'sub')), parts along dimension 0, may hold values from -6 to 6
- query_heads: bfloat16 [4, 2048, 1024], P(('groups', 'fsdp'), ('ctx', 'sub')), parts along dimension 0, may hold values from -11 to 11
- key_heads: bfloat16 [4, 2048, 512], P(('groups', 'fsdp'), ('ctx', 'sub')), parts along dimension 0, may hold values from -11 to 11
- value_heads: bfloat16 [4, 2048, 512], P(('groups', 'fsdp'), ('ctx', 'sub')), parts along dimension 0, may hold values from -6 to 6
- grad_out: bfloat16 [4, 2048, 1024], P(('groups', 'fsdp'), ('ctx', 'sub')), parts along dimension 0, may hold values from -96 to 96
- doc_starts: int32 [4, 12], P(('groups', 'fsdp')), parts along dimension 0, may hold values from 0 to 2047, as said below
Outputs:
- grad_query: bfloat16 [4, 2048, 1024], P(('groups', 'fsdp'), ('ctx', 'sub')), parts along dimension 0
- grad_key: bfloat16 [4, 2048, 512], P(('groups', 'fsdp'), ('ctx', 'sub')), parts along dimension 0
- grad_value: bfloat16 [4, 2048, 512], P(('groups', 'fsdp'), ('ctx', 'sub')), parts along dimension 0
- grad_value_proj: float32 [4608, 512], P(('groups', 'fsdp')), parts along dimension 0
There are 2 independent parts, one for each index of `groups`. A program takes and returns all parts, laid end to end along the dimension named above; each array names one. Nothing has to cross between parts.
Inputs may be any that keep to these rules, and one draw needn't show every extreme that they name: `doc_starts`: each row holds the first positions of the 12 documents of one sequence in increasing order; the first is 0, every document has at least one token, and the longest has exactly 1024 tokens.
All inputs are finite; a program needn't handle non-finite values.
Results may differ from a plain program's by a relative error of at most 0.015.
Values may be sent and summed in bfloat16 or wider, within the bound.
No kernel may reach another device: no remote copies, remote signals or barrier semaphores. Data moves between devices by JAX's collectives and lax.ppermute only.
A program may use at most 64 MiB of HBM per device.

v0:
```python
import jax
import jax.numpy as jnp
from jax import lax
from jax.sharding import PartitionSpec as P

HEAD_DIM = 256
SPAN = 768


def passed_along(value, axis, steps):
    count = lax.axis_size(axis)
    first, last = (max(0, -steps), min(count, count - steps))
    return lax.ppermute(value, axis, [(source, source + steps) for source in range(first, last)])


def doc_start_of(starts, positions):
    covered = starts[None, :] <= positions[:, None]
    return jnp.max(jnp.where(covered, starts[None, :], 0), axis=1)


def attend_block(queries, key_block, value_block, grads, query_pos, key_pos, lowest):
    row_count = queries.shape[0]
    key_count = key_block.shape[0]
    groups = key_block.shape[1] // HEAD_DIM
    per_group = queries.shape[1] // key_block.shape[1]
    inv_root = HEAD_DIM ** (-0.5)
    query_four = queries.reshape(row_count, groups, per_group, HEAD_DIM)
    grad_four = grads.reshape(row_count, groups, per_group, HEAD_DIM)
    key_three = key_block.reshape(key_count, groups, HEAD_DIM)
    value_three = value_block.reshape(key_count, groups, HEAD_DIM)
    allowed = (key_pos[None, :] >= lowest[:, None]) & (key_pos[None, :] <= query_pos[:, None])

    def one_group(group):
        query_g = lax.dynamic_index_in_dim(query_four, group, 1, keepdims=False)
        grad_g = lax.dynamic_index_in_dim(grad_four, group, 1, keepdims=False)
        key_g = lax.dynamic_index_in_dim(key_three, group, 1, keepdims=False)
        value_g = lax.dynamic_index_in_dim(value_three, group, 1, keepdims=False)
        scores = (
            jnp.einsum("thd,kd->htk", query_g, key_g, preferred_element_type=jnp.float32) * inv_root
        )
        scores = jnp.where(allowed[None], scores, -1e30)
        largest = jnp.max(scores, axis=2, keepdims=True)
        raised = jnp.where(allowed[None], jnp.exp(scores - largest), 0.0)
        attn_probs = raised / jnp.sum(raised, axis=2, keepdims=True)
        grad_probs = jnp.einsum("thd,kd->htk", grad_g, value_g, preferred_element_type=jnp.float32)
        row_dot = jnp.sum(attn_probs * grad_probs, axis=2, keepdims=True)
        grad_scores = (attn_probs * (grad_probs - row_dot) * inv_root).astype(jnp.bfloat16)
        probs_low = attn_probs.astype(jnp.bfloat16)
        grad_q = jnp.einsum("htk,kd->thd", grad_scores, key_g, preferred_element_type=jnp.float32)
        grad_k = jnp.einsum("htk,thd->kd", grad_scores, query_g, preferred_element_type=jnp.float32)
        grad_v = jnp.einsum("htk,thd->kd", probs_low, grad_g, preferred_element_type=jnp.float32)
        return (grad_q, grad_k, grad_v)

    grad_q, grad_k, grad_v = lax.map(one_group, jnp.arange(groups, dtype=jnp.int32))
    grad_q = jnp.moveaxis(grad_q, 0, 1).reshape(row_count, -1)
    grad_k = jnp.moveaxis(grad_k, 0, 1).reshape(key_count, -1)
    grad_v = jnp.moveaxis(grad_v, 0, 1).reshape(key_count, -1)
    return (grad_q, grad_k, grad_v)


def body(layer_input, query_heads, key_heads, value_heads, grad_out, doc_starts):
    block_rows = query_heads.shape[1]
    window = min(SPAN, lax.axis_size(("ctx", "sub")) * block_rows // 2)
    reach_blocks = (window + block_rows - 2) // block_rows
    margin_rows = reach_blocks * block_rows
    key_count = margin_rows + block_rows
    first_row = lax.axis_index(("ctx", "sub")) * block_rows
    own_keys = key_heads[0]
    own_values = value_heads[0]
    arrived = []
    moving_k = own_keys
    moving_v = own_values
    for distance in range(reach_blocks):
        moving_k, moving_v = passed_along((moving_k, moving_v), ("ctx", "sub"), 1)
        arrived.append((moving_k, moving_v))
    arrived = arrived[::-1]
    key_span = jnp.concatenate([pair[0] for pair in arrived] + [own_keys], axis=0)
    value_span = jnp.concatenate([pair[1] for pair in arrived] + [own_values], axis=0)
    query_pos = first_row + jnp.arange(block_rows, dtype=jnp.int32)
    key_pos = first_row - margin_rows + jnp.arange(key_count, dtype=jnp.int32)
    lowest = jnp.maximum(doc_start_of(doc_starts[0], query_pos), query_pos - window + 1)
    grad_q, grad_k_span, grad_v_span = attend_block(
        query_heads[0], key_span, value_span, grad_out[0], query_pos, key_pos, lowest
    )

    def own_piece(distance):
        begin = (reach_blocks - distance) * block_rows
        return (grad_k_span[begin : begin + block_rows], grad_v_span[begin : begin + block_rows])

    total_k, total_v = own_piece(reach_blocks)
    for distance in range(reach_blocks - 1, -1, -1):
        moved_k, moved_v = (
            passed_along(total_k.astype(jnp.bfloat16), ("ctx", "sub"), -1).astype(total_k.dtype),
            passed_along(total_v.astype(jnp.bfloat16), ("ctx", "sub"), -1).astype(total_v.dtype),
        )
        piece_k, piece_v = own_piece(distance)
        total_k = moved_k + piece_k
        total_v = moved_v + piece_v
    grad_key = total_k.astype(jnp.bfloat16)
    grad_value = total_v.astype(jnp.bfloat16)
    contract = (((0,), (0,)), ((), ()))
    term_v = lax.dot_general(
        layer_input[0], grad_value, contract, preferred_element_type=jnp.float32
    )
    shard_v = lax.psum_scatter(term_v.astype(jnp.bfloat16), "fsdp", scatter_dimension=0, tiled=True)
    weight_v = lax.psum(shard_v, ("ctx", "sub")).astype(jnp.float32)
    token_scale = float(lax.axis_size("fsdp") * lax.axis_size(("ctx", "sub")) * block_rows) ** (
        -0.5
    )
    return (
        grad_q.astype(jnp.bfloat16)[None],
        grad_key[None],
        grad_value[None],
        weight_v * token_scale,
    )


def solution(mesh):
    placed = (
        P(("groups", "fsdp"), ("ctx", "sub"), None),
        P(("groups", "fsdp"), ("ctx", "sub"), None),
        P(("groups", "fsdp"), ("ctx", "sub"), None),
        P(("groups", "fsdp"), ("ctx", "sub"), None),
        P(("groups", "fsdp"), ("ctx", "sub"), None),
        P(("groups", "fsdp"), None),
    )
    return jax.shard_map(
        body,
        mesh=mesh,
        in_specs=placed,
        out_specs=(
            P(("groups", "fsdp"), ("ctx", "sub"), None),
            P(("groups", "fsdp"), ("ctx", "sub"), None),
            P(("groups", "fsdp"), ("ctx", "sub"), None),
            P(("groups", "fsdp"), None),
        ),
        check_vma=False,
    )
```

profile of v0, /device:TPU:0, one launch (start us, length us, event | category | flops | bytes accessed | tf_op | source)
XLA Modules:
  0.0 211.9 jit_solution(1971740638180802092)
XLA Ops:
  7.2 1.2 copy.68
  8.4 2.4 %collective-permute-start = (bf16[256,512]{0,1:T(8,128)(2,1)S(1)}, bf16[256,512]{0,1:T(8,128)(2,1)S(1)}, u32[]{:S(2)}, u32[]{:S(2)}) collective-permute-start(bf16[256,512]{0,1:T(8,128)(2,1)S(1)} %bitcast.186), channel_id=1, source_target_pairs={{0,1},{1,4},{4,5},{5,8},{8,9},{9,12},{12,13},{2,3},{3,6},{6,7},{7,... | collective-permute-start | bytes 786440 | tf_op jit(solution)/shard_map/ppermute | solution.py:13
  10.8 1.1 copy.71
  11.9 4.6 %collective-permute-start.3 = (bf16[256,512]{0,1:T(8,128)(2,1)S(1)}, bf16[256,512]{0,1:T(8,128)(2,1)S(1)}, u32[]{:S(2)}, u32[]{:S(2)}) collective-permute-start(bf16[256,512]{0,1:T(8,128)(2,1)S(1)} %bitcast.184), channel_id=1, source_target_pairs={{0,1},{1,4},{4,5},{5,8},{8,9},{9,12},{12,13},{2,3},{3,6},{6,7},{7,... | collective-permute-start | bytes 786440 | tf_op jit(solution)/shard_map/ppermute | solution.py:13
  16.5 2.2 %collective-permute-start.1 = (bf16[256,512]{0,1:T(8,128)(2,1)S(1)}, bf16[256,512]{0,1:T(8,128)(2,1)S(1)}, u32[]{:S(2)}, u32[]{:S(2)}) collective-permute-start(bf16[256,512]{0,1:T(8,128)(2,1)S(1)} %collective-permute-done), channel_id=1, source_target_pairs={{0,1},{1,4},{4,5},{5,8},{8,9},{9,12},{12,13},{2,3},{3,6},{6,7},{7,... | collective-permute-start | bytes 786440 | tf_op jit(solution)/shard_map/ppermute | solution.py:13
  18.7 4.4 %collective-permute-start.4 = (bf16[256,512]{0,1:T(8,128)(2,1)S(1)}, bf16[256,512]{0,1:T(8,128)(2,1)S(1)}, u32[]{:S(2)}, u32[]{:S(2)}) collective-permute-start(bf16[256,512]{0,1:T(8,128)(2,1)S(1)} %collective-permute-done.3), channel_id=1, source_target_pairs={{0,1},{1,4},{4,5},{5,8},{8,9},{9,12},{12,13},{2,3},{3,6},{6,7},{7,... | collective-permute-start | bytes 786440 | tf_op jit(solution)/shard_map/ppermute | solution.py:13
  23.9 3.7 %collective-permute-start.2 = (bf16[256,512]{0,1:T(8,128)(2,1)S(1)}, bf16[256,512]{0,1:T(8,128)(2,1)}, u32[]{:S(2)}, u32[]{:S(2)}) collective-permute-start(bf16[256,512]{0,1:T(8,128)(2,1)S(1)} %collective-permute-done.1), channel_id=1, source_target_pairs={{0,1},{1,4},{4,5},{5,8},{8,9},{9,12},{12,13},{2,3},{3,6},{6,7},{7,... | collective-permute-start | bytes 786440 | tf_op jit(solution)/shard_map/ppermute | solution.py:13
  27.6 3.2 %collective-permute-start.5 = (bf16[256,512]{0,1:T(8,128)(2,1)S(1)}, bf16[256,512]{0,1:T(8,128)(2,1)S(1)}, u32[]{:S(2)}, u32[]{:S(2)}) collective-permute-start(bf16[256,512]{0,1:T(8,128)(2,1)S(1)} %collective-permute-done.4), channel_id=1, source_target_pairs={{0,1},{1,4},{4,5},{5,8},{8,9},{9,12},{12,13},{2,3},{3,6},{6,7},{7,... | collective-permute-start | bytes 786440 | tf_op jit(solution)/shard_map/ppermute | solution.py:13
  30.8 2.1 copy.73
  32.9 1.0 copy.70
  33.9 2.1 pad_maximum_fusion
  36.0 1.2 pad_maximum_fusion.1
  37.1 37.4 %while.15 = (s32[]{:T(128)}, bf16[2,256,2,256]{1,3,2,0:T(8,128)(2,1)}, f32[2,1024,256]{2,1,0:T(8,128)}, f32[2,1024,256]{2,1,0:T(8,128)}, s32[2]{0:T(128)S(1)}, /...) while((s32[]{:T(128)}, ...), condition=%wide.region_5.6_spmd.clone, body=%wide.region_1.5_spmd.clone.sunk | while | flops 1353977856 | bytes 29120200 | solution.py:54
  39.9 3.5 %fusion.90 = (f32[2,256]{1,0:T(2,128)S(1)}, f32[2,256,1024]{1,2,0:T(8,128)}) fusion(pred[256,1024]{0,1:T(8,128)(4,1)S(1)} %compare_and_fusion.2, bf16[256,2,2,256]{0,3,2,1:T(8,128)(2,1)} %get-tuple-element.287, s32[]{:T(128)S(6)} %select_n.34, bf16[1024,2,256]{0,2,1:T(8,128)(2,1)} %get-tuple-element.286), kind=kOutput, calls=%fused_computation.80.clone.1 | convolution fusion | flops 271057920 | bytes 3410944 | tf_op jit(solution)/shard_map/while/body/eval_jaxpr/sub | solution.py:43
  43.4 1.6 fusion.89
  45.0 3.9 %fusion.92 = f32[2,1024,256]{2,1,0:T(8,128)} fusion(f32[2,1024,256]{2,1,0:T(8,128)} %get-tuple-element.268, s32[]{:T(128)} %get-tuple-element.266, f32[1024,256,2]{1,0,2:T(8,128)S(1)} %fusion.89, bf16[256,2,2,256]{0,3,2,1:T(8,128)(2,1)} %get-tuple-element.287, s32[]{:T(128)S(6)} %select_n.34, f32[2,256,1024]{1,2,0:T(8,128)} %get-tuple-element.249, ...), kind=kOutput, calls=%fused_computation.14.clone.1 | convolution fusion | flops 272107008 | bytes 9703940 | tf_op jit(solution)/shard_map/while/body/eval_jaxpr/htk,thd->kd/dot_general | solution.py:50
  48.9 3.0 %fusion.93 = f32[2,1024,256]{2,1,0:T(8,128)} fusion(f32[2,1024,256]{2,1,0:T(8,128)} %get-tuple-element.269, s32[]{:T(128)} %get-tuple-element.266, bf16[256,2,2,256]{0,3,2,1:T(8,128)(2,1)} %get-tuple-element.289, s32[]{:T(128)S(6)} %select_n.34, f32[2,256,1024]{1,2,0:T(8,128)} %get-tuple-element.249, f32[2,256]{1,0:T(2,128)S(1)} %get-tuple-element.250), kind=kOutput, calls=%fused_computation.12.clone.1 | convolution fusion | flops 269484032 | bytes 3410436 | tf_op jit(solution)/shard_map/while/body/eval_jaxpr/htk,thd->kd/dot_general | solution.py:51
  51.9 3.9 %fusion.91 = bf16[2,256,2,256]{1,3,2,0:T(8,128)(2,1)} fusion(bf16[2,256,2,256]{1,3,2,0:T(8,128)(2,1)} %get-tuple-element.267, s32[]{:T(128)} %get-tuple-element.266, f32[1024,256,2]{1,0,2:T(8,128)S(1)} %fusion.89, bf16[1024,2,256]{0,2,1:T(8,128)(2,1)} %get-tuple-element.286, s32[]{:T(128)S(6)} %select_n.34, f32[2,256,1024]{1,2,0:T(8,128)} %get-tuple-element.249, ...), kind=kOutput, calls=%fused_computation.16.clone.1 | convolution fusion | flops 272107008 | bytes 9441796 | tf_op jit(solution)/shard_map/while/body/eval_jaxpr/htk,kd->thd/dot_general | solution.py:49
  58.6 3.5 %fusion.90 = (f32[2,256]{1,0:T(2,128)S(1)}, f32[2,256,1024]{1,2,0:T(8,128)}) fusion(pred[256,1024]{0,1:T(8,128)(4,1)S(1)} %compare_and_fusion.2, bf16[256,2,2,256]{0,3,2,1:T(8,128)(2,1)} %get-tuple-element.287, s32[]{:T(128)S(6)} %select_n.34, bf16[1024,2,256]{0,2,1:T(8,128)(2,1)} %get-tuple-element.286), kind=kOutput, calls=%fused_computation.80.clone.1 | convolution fusion | flops 271057920 | bytes 3410944 | tf_op jit(solution)/shard_map/while/body/eval_jaxpr/sub | solution.py:43
  62.1 1.6 fusion.89
  63.6 4.0 %fusion.92 = f32[2,1024,256]{2,1,0:T(8,128)} fusion(f32[2,1024,256]{2,1,0:T(8,128)} %get-tuple-element.268, s32[]{:T(128)} %get-tuple-element.266, f32[1024,256,2]{1,0,2:T(8,128)S(1)} %fusion.89, bf16[256,2,2,256]{0,3,2,1:T(8,128)(2,1)} %get-tuple-element.287, s32[]{:T(128)S(6)} %select_n.34, f32[2,256,1024]{1,2,0:T(8,128)} %get-tuple-element.249, ...), kind=kOutput, calls=%fused_computation.14.clone.1 | convolution fusion | flops 272107008 | bytes 9703940 | tf_op jit(solution)/shard_map/while/body/eval_jaxpr/htk,thd->kd/dot_general | solution.py:50
  67.6 3.0 %fusion.93 = f32[2,1024,256]{2,1,0:T(8,128)} fusion(f32[2,1024,256]{2,1,0:T(8,128)} %get-tuple-element.269, s32[]{:T(128)} %get-tuple-element.266, bf16[256,2,2,256]{0,3,2,1:T(8,128)(2,1)} %get-tuple-element.289, s32[]{:T(128)S(6)} %select_n.34, f32[2,256,1024]{1,2,0:T(8,128)} %get-tuple-element.249, f32[2,256]{1,0:T(2,128)S(1)} %get-tuple-element.250), kind=kOutput, calls=%fused_computation.12.clone.1 | convolution fusion | flops 269484032 | bytes 3410436 | tf_op jit(solution)/shard_map/while/body/eval_jaxpr/htk,thd->kd/dot_general | solution.py:51
  70.7 3.9 %fusion.91 = bf16[2,256,2,256]{1,3,2,0:T(8,128)(2,1)} fusion(bf16[2,256,2,256]{1,3,2,0:T(8,128)(2,1)} %get-tuple-element.267, s32[]{:T(128)} %get-tuple-element.266, f32[1024,256,2]{1,0,2:T(8,128)S(1)} %fusion.89, bf16[1024,2,256]{0,2,1:T(8,128)(2,1)} %get-tuple-element.286, s32[]{:T(128)S(6)} %select_n.34, f32[2,256,1024]{1,2,0:T(8,128)} %get-tuple-element.249, ...), kind=kOutput, calls=%fused_computation.16.clone.1 | convolution fusion | flops 272107008 | bytes 9441796 | tf_op jit(solution)/shard_map/while/body/eval_jaxpr/htk,kd->thd/dot_general | solution.py:49
  74.5 1.1 fusion.61
  75.6 1.3 collective-permute-start.9
  76.9 1.5 slice_bitcast_fusion.2
  78.5 1.2 collective-permute-done.9
  79.7 1.3 collective-permute-start.10
  81.1 6.3 %collective-permute-done.10 = bf16[256,512]{1,0:T(8,128)(2,1)S(1)} collective-permute-done((bf16[256,512]{1,0:T(8,128)(2,1)S(1)}, bf16[256,512]{1,0:T(8,128)(2,1)S(1)}, u32[]{:S(2)}, u32[]{:S(2)}) %collective-permute-start.10) | collective-permute-done | bytes 262176 | tf_op jit(solution)/shard_map/ppermute | solution.py:13
  87.5 1.3 collective-permute-start.11
  88.9 6.3 %collective-permute-done.11 = bf16[256,512]{1,0:T(8,128)(2,1)S(1)} collective-permute-done((bf16[256,512]{1,0:T(8,128)(2,1)S(1)}, bf16[256,512]{1,0:T(8,128)(2,1)S(1)}, u32[]{:S(2)}, u32[]{:S(2)}) %collective-permute-start.11) | collective-permute-done | bytes 262176 | tf_op jit(solution)/shard_map/ppermute | solution.py:13
  95.9 0.8 fusion.57
  96.7 2.4 %copy.92 = bf16[2304,512]{1,0:T(8,128)(2,1)} copy(bf16[2304,512]{0,1:T(8,128)(2,1)S(1)} %fusion.57) | data formatting | bytes 4718592
  99.2 1.1 fusion.60
  100.4 1.3 collective-permute-start.6
  101.7 1.5 slice_bitcast_fusion.5
  103.2 4.9 %collective-permute-done.6 = bf16[256,512]{1,0:T(8,128)(2,1)S(1)} collective-permute-done((bf16[256,512]{1,0:T(8,128)(2,1)S(1)}, bf16[256,512]{1,0:T(8,128)(2,1)S(1)}, u32[]{:S(2)}, u32[]{:S(2)}) %collective-permute-start.6) | collective-permute-done | bytes 262176 | tf_op jit(solution)/shard_map/ppermute | solution.py:13
  108.0 0.8 add_convert_fusion.5
  108.8 1.3 collective-permute-start.7
  110.2 28.5 %reduce-scatter.4.cloned.1.call-done = bf16[1152,512]{1,0:T(8,128)(2,1)} async-done(((bf16[2304,512]{1,0:T(8,128)(2,1)}), bf16[1152,512]{1,0:T(8,128)(2,1)}) %reduce-scatter.4.cloned.1.call-update) | async-done | bytes 1179664
  138.7 2.4 %copy.93 = bf16[1152,512]{0,1:T(8,128)(2,1)} copy(bf16[1152,512]{1,0:T(8,128)(2,1)} %reduce-scatter.4.cloned.1.call-done) | data formatting | bytes 2359296
  141.1 1.8 add_convert_fusion.4
  142.9 1.3 collective-permute-start.8
  144.3 1.0 copy.90
  146.7 1.7 fusion.59
  148.4 53.2 %all-reduce.2.cloned.1.call-done = bf16[1152,512]{0,1:T(8,128)(2,1)} async-done(((bf16[1152,512]{0,1:T(8,128)(2,1)}), bf16[1152,512]{0,1:T(8,128)(2,1)}) %all-reduce.2.cloned.1.call-update) | async-done | bytes 1179664 | tf_op jit(solution)/shard_map/psum | solution.py:106
  201.6 1.4 convert_multiply_fusion
  203.1 2.0 copy.87
  (49 shorter events, 5.2 us)
Async XLA Ops:
  7.2 88.7 %copy-start = (bf16[1,256,2304]{2,1,0:T(8,128)(2,1)S(1)}, bf16[1,256,2304]{2,1,0:T(8,128)(2,1)}, u32[]{:S(2)}) copy-start(bf16[1,256,2304]{2,1,0:T(8,128)(2,1)} %param.8) | copy-start | bytes 3538948
  7.2 25.7 %copy-start.5 = (bf16[1,256,1024]{2,1,0:T(8,128)(2,1)S(1)}, bf16[1,256,1024]{2,1,0:T(8,128)(2,1)}, u32[]{:S(2)}) copy-start(bf16[1,256,1024]{2,1,0:T(8,128)(2,1)} %param.9) | copy-start | bytes 1572868
  7.2 131.5 %reduce-scatter.4.cloned.1.call-start = ((), (), s32[]{:S(2)}) async-start(), calls=%async_computation.2 | async-start | bytes 3538944
  8.4 8.1 %collective-permute-start = (bf16[256,512]{0,1:T(8,128)(2,1)S(1)}, bf16[256,512]{0,1:T(8,128)(2,1)S(1)}, u32[]{:S(2)}, u32[]{:S(2)}) collective-permute-start(bf16[256,512]{0,1:T(8,128)(2,1)S(1)} %bitcast.186), channel_id=1, source_target_pairs={{0,1},{1,4},{4,5},{5,8},{8,9},{9,12},{12,13},{2,3},{3,6},{6,7},{7,... | collective-permute-start | bytes 786440 | tf_op jit(solution)/shard_map/ppermute | solution.py:13
  11.9 6.8 %collective-permute-start.3 = (bf16[256,512]{0,1:T(8,128)(2,1)S(1)}, bf16[256,512]{0,1:T(8,128)(2,1)S(1)}, u32[]{:S(2)}, u32[]{:S(2)}) collective-permute-start(bf16[256,512]{0,1:T(8,128)(2,1)S(1)} %bitcast.184), channel_id=1, source_target_pairs={{0,1},{1,4},{4,5},{5,8},{8,9},{9,12},{12,13},{2,3},{3,6},{6,7},{7,... | collective-permute-start | bytes 786440 | tf_op jit(solution)/shard_map/ppermute | solution.py:13
  16.5 7.4 %collective-permute-start.1 = (bf16[256,512]{0,1:T(8,128)(2,1)S(1)}, bf16[256,512]{0,1:T(8,128)(2,1)S(1)}, u32[]{:S(2)}, u32[]{:S(2)}) collective-permute-start(bf16[256,512]{0,1:T(8,128)(2,1)S(1)} %collective-permute-done), channel_id=1, source_target_pairs={{0,1},{1,4},{4,5},{5,8},{8,9},{9,12},{12,13},{2,3},{3,6},{6,7},{7,... | collective-permute-start | bytes 786440 | tf_op jit(solution)/shard_map/ppermute | solution.py:13
  18.7 8.9 %collective-permute-start.4 = (bf16[256,512]{0,1:T(8,128)(2,1)S(1)}, bf16[256,512]{0,1:T(8,128)(2,1)S(1)}, u32[]{:S(2)}, u32[]{:S(2)}) collective-permute-start(bf16[256,512]{0,1:T(8,128)(2,1)S(1)} %collective-permute-done.3), channel_id=1, source_target_pairs={{0,1},{1,4},{4,5},{5,8},{8,9},{9,12},{12,13},{2,3},{3,6},{6,7},{7,... | collective-permute-start | bytes 786440 | tf_op jit(solution)/shard_map/ppermute | solution.py:13
  23.9 10.0 %collective-permute-start.2 = (bf16[256,512]{0,1:T(8,128)(2,1)S(1)}, bf16[256,512]{0,1:T(8,128)(2,1)}, u32[]{:S(2)}, u32[]{:S(2)}) collective-permute-start(bf16[256,512]{0,1:T(8,128)(2,1)S(1)} %collective-permute-done.1), channel_id=1, source_target_pairs={{0,1},{1,4},{4,5},{5,8},{8,9},{9,12},{12,13},{2,3},{3,6},{6,7},{7,... | collective-permute-start | bytes 786440 | tf_op jit(solution)/shard_map/ppermute | solution.py:13
  27.6 8.4 %collective-permute-start.5 = (bf16[256,512]{0,1:T(8,128)(2,1)S(1)}, bf16[256,512]{0,1:T(8,128)(2,1)S(1)}, u32[]{:S(2)}, u32[]{:S(2)}) collective-permute-start(bf16[256,512]{0,1:T(8,128)(2,1)S(1)} %collective-permute-done.4), channel_id=1, source_target_pairs={{0,1},{1,4},{4,5},{5,8},{8,9},{9,12},{12,13},{2,3},{3,6},{6,7},{7,... | collective-permute-start | bytes 786440 | tf_op jit(solution)/shard_map/ppermute | solution.py:13
  75.6 4.0 %collective-permute-start.9 = (bf16[256,512]{1,0:T(8,128)(2,1)S(1)}, bf16[256,512]{1,0:T(8,128)(2,1)S(1)}, u32[]{:S(2)}, u32[]{:S(2)}) collective-permute-start(bf16[256,512]{1,0:T(8,128)(2,1)S(1)} %bitcast.189), channel_id=1, source_target_pairs={{1,0},{4,1},{5,4},{8,5},{9,8},{12,9},{13,12},{3,2},{6,3},{7,6},{10... | collective-permute-start | bytes 786440 | tf_op jit(solution)/shard_map/ppermute | solution.py:13
  79.7 7.7 %collective-permute-start.10 = (bf16[256,512]{1,0:T(8,128)(2,1)S(1)}, bf16[256,512]{1,0:T(8,128)(2,1)S(1)}, u32[]{:S(2)}, u32[]{:S(2)}) collective-permute-start(bf16[256,512]{1,0:T(8,128)(2,1)S(1)} %add_convert_fusion.2), channel_id=1, source_target_pairs={{1,0},{4,1},{5,4},{8,5},{9,8},{12,9},{13,12},{3,2},{6,3},{7,6},{10... | collective-permute-start | bytes 786440 | tf_op jit(solution)/shard_map/ppermute | solution.py:13
  87.5 7.7 %collective-permute-start.11 = (bf16[256,512]{1,0:T(8,128)(2,1)S(1)}, bf16[256,512]{1,0:T(8,128)(2,1)S(1)}, u32[]{:S(2)}, u32[]{:S(2)}) collective-permute-start(bf16[256,512]{1,0:T(8,128)(2,1)S(1)} %add_convert_fusion.1), channel_id=1, source_target_pairs={{1,0},{4,1},{5,4},{8,5},{9,8},{12,9},{13,12},{3,2},{6,3},{7,6},{10... | collective-permute-start | bytes 786440 | tf_op jit(solution)/shard_map/ppermute | solution.py:13
  88.9 6.3 %copy-start.1 = (f32[2,32,8,256]{3,2,0,1:T(8,128)}, f32[2,32,8,256]{3,2,0,1:T(8,128)S(1)}, u32[]{:S(2)}) copy-start(f32[2,32,8,256]{3,2,0,1:T(8,128)S(1)} %copy.105) | copy-start | bytes 1572868
  95.2 0.7 copy-start.3
  99.2 102.4 %all-reduce.2.cloned.1.call-start = ((), (), s32[]{:S(2)}) async-start(), calls=%async_computation.1 | async-start | bytes 2359296 | tf_op jit(solution)/shard_map/psum | solution.py:106
  100.4 7.7 %collective-permute-start.6 = (bf16[256,512]{1,0:T(8,128)(2,1)S(1)}, bf16[256,512]{1,0:T(8,128)(2,1)S(1)}, u32[]{:S(2)}, u32[]{:S(2)}) collective-permute-start(bf16[256,512]{1,0:T(8,128)(2,1)S(1)} %bitcast.190), channel_id=1, source_target_pairs={{1,0},{4,1},{5,4},{8,5},{9,8},{12,9},{13,12},{3,2},{6,3},{7,6},{10... | collective-permute-start | bytes 786440 | tf_op jit(solution)/shard_map/ppermute | solution.py:13
  108.8 32.3 %collective-permute-start.7 = (bf16[256,512]{1,0:T(8,128)(2,1)}, bf16[256,512]{1,0:T(8,128)(2,1)}, u32[]{:S(2)}, u32[]{:S(2)}) collective-permute-start(bf16[256,512]{1,0:T(8,128)(2,1)} %add_convert_fusion.5), channel_id=1, source_target_pairs={{1,0},{4,1},{5,4},{8,5},{9,8},{12,9},{13,12},{3,2},{6,3},{7,6},{10... | collective-permute-start | bytes 786440 | tf_op jit(solution)/shard_map/ppermute | solution.py:13
  141.1 3.2 %copy-start.6 = (bf16[2,256,2,256]{1,3,2,0:T(8,128)(2,1)S(1)}, bf16[2,256,2,256]{1,3,2,0:T(8,128)(2,1)}, u32[]{:S(2)}) copy-start(bf16[2,256,2,256]{1,3,2,0:T(8,128)(2,1)} %get-tuple-element.58) | copy-start | bytes 1572868
  141.1 4.2 %copy-start.2 = (f32[2,32,8,256]{3,2,0,1:T(8,128)S(1)}, f32[2,32,8,256]{3,2,0,1:T(8,128)}, u32[]{:S(2)}) copy-start(f32[2,32,8,256]{3,2,0,1:T(8,128)} %copy-done.1) | copy-start | bytes 1572868
  141.1 4.2 %copy-start.4 = (bf16[256,512]{1,0:T(8,128)(2,1)S(1)}, bf16[256,512]{1,0:T(8,128)(2,1)}, u32[]{:S(2)}) copy-start(bf16[256,512]{1,0:T(8,128)(2,1)} %copy-done.3) | copy-start | bytes 786436
  142.9 3.8 %collective-permute-start.8 = (bf16[256,512]{1,0:T(8,128)(2,1)}, bf16[256,512]{1,0:T(8,128)(2,1)}, u32[]{:S(2)}, u32[]{:S(2)}) collective-permute-start(bf16[256,512]{1,0:T(8,128)(2,1)} %add_convert_fusion.4), channel_id=1, source_target_pairs={{1,0},{4,1},{5,4},{8,5},{9,8},{12,9},{13,12},{3,2},{6,3},{7,6},{10... | collective-permute-start | bytes 786440 | tf_op jit(solution)/shard_map/ppermute | solution.py:13
Sparse Core Ops, SparseCore 0:
  99.3 39.3 reduce-scatter.3
  141.7 59.8 all-reduce.1
where the time goes:
time: 213 us; the launch traced here: 212 us
  waiting for transfers between devices  101 us (47%)
  matrix products  32.6 us (15%)
  starting transfers between devices  28.2 us (13%)
  local copies, waits for them, and re-layouts  20.5 us (10%)
  between operations  14.4 us (7%)
  other arithmetic  11.2 us (5%)
  loops' own time  3.92 us (2%)
    psum x1, waiting for transfers between devices, body(): weight_v = lax.psum(shard_v, ('ctx', 'sub')).astype(jnp.float32)  53.2 us
    unnamed x3, waiting for transfers between devices  28.5 us
    ppermute x12, starting transfers between devices, passed_along(): lax.ppermute(value, axis, [(source, source + steps) for source in range(f...  28.2 us
    ppermute x12, waiting for transfers between devices, passed_along(): lax.ppermute(value, axis, [(source, source + steps) for source in range(f...  19.3 us
    unnamed x25, local copies, waits for them, and re-layouts  17.9 us
    dot_general x2, matrix products, one_group(): jnp.einsum('htk,thd->kd', grad_scores, query_g, preferred_element_type=jn...  7.91 us
    dot_general x2, matrix products, one_group(): jnp.einsum('htk,kd->thd', grad_scores, key_g, preferred_element_type=jnp....  7.74 us
    sub x2, matrix products, one_group(): raised = jnp.where(allowed[None], jnp.exp(scores - largest), 0.0)  6.91 us
  transfers between devices with their start and end apart: 14, of which 7 were waited for; matrix products, arithmetic and copies ran while one was open for 9% of the time, Pallas kernels for 0%

commit v1 on v0

--- a/solution.py
+++ b/solution.py
@@ -5,6 +5,11 @@
 
 HEAD_DIM = 256
 SPAN = 768
+
+
+def add_all(block, mesh_axis):
+    parts = lax.all_gather(block, mesh_axis)
+    return jnp.sum(parts, axis=0)
 
 
 def passed_along(value, axis, steps):
@@ -103,7 +108,7 @@
         layer_input[0], grad_value, contract, preferred_element_type=jnp.float32
     )
     shard_v = lax.psum_scatter(term_v.astype(jnp.bfloat16), "fsdp", scatter_dimension=0, tiled=True)
-    weight_v = lax.psum(shard_v, ("ctx", "sub")).astype(jnp.float32)
+    weight_v = add_all(shard_v, ("ctx", "sub")).astype(jnp.float32)
     token_scale = float(lax.axis_size("fsdp") * lax.axis_size(("ctx", "sub")) * block_rows) ** (
         -0.5
     )

time: 213 us -> 267 us (1.25)
  waiting for transfers between devices: 101 us -> 139 us
  local copies, waits for them, and re-layouts: 20.5 us -> 29.3 us
  other arithmetic: 11.2 us -> 18.8 us
    all_gather x0 -> x1, waiting for transfers between devices: none -> 65.9 us  [add_all(): parts = lax.all_gather(block, mesh_axis)]
    psum x1 -> x0, waiting for transfers between devices: 53.2 us -> none  [body(): weight_v = lax.psum(shard_v, ('ctx', 'sub')).astype(jnp.float32)]
    ppermute x12, waiting for transfers between devices: 19.3 us -> 33.8 us  [passed_along(): lax.ppermute(value, axis, [(source, source + steps) for source in range(f...]
    reduce_sum x0 -> x1, other arithmetic: none -> 11 us  [add_all(): return jnp.sum(parts, axis=0)]
    unnamed x3, waiting for transfers between devices: 28.5 us -> 39.5 us
    unnamed x25 -> x26, local copies, waits for them, and re-layouts: 17.9 us -> 26.6 us
  transfers between devices with their start and end apart: 14 -> 14, of which waited for: 7 -> 8; matrix products, arithmetic and copies ran while one was open for 9% -> 5% of each run, Pallas kernels for 0% -> 0%
where the time goes in v1:
time: 267 us; the launch traced here: 266 us
  waiting for transfers between devices  139 us (52%)
  matrix products  30.7 us (11%)
  local copies, waits for them, and re-layouts  29.3 us (11%)
  starting transfers between devices  29.3 us (11%)
  other arithmetic  18.8 us (7%)
  between operations  14.4 us (5%)
  loops' own time  3.96 us (1%)
    all_gather x1, waiting for transfers between devices, add_all(): parts = lax.all_gather(block, mesh_axis)  65.9 us
    unnamed x3, waiting for transfers between devices  39.5 us
    ppermute x12, waiting for transfers between devices, passed_along(): lax.ppermute(value, axis, [(source, source + steps) for source in range(f...  33.8 us
    ppermute x12, starting transfers between devices, passed_along(): lax.ppermute(value, axis, [(source, source + steps) for source in range(f...  29.2 us
    unnamed x26, local copies, waits for them, and re-layouts  26.6 us
    reduce_sum x1, other arithmetic, add_all(): return jnp.sum(parts, axis=0)  11 us
    dot_general x2, matrix products, one_group(): jnp.einsum('htk,thd->kd', grad_scores, query_g, preferred_element_type=jn...  7.86 us
    dot_general x2, matrix products, one_group(): jnp.einsum('htk,kd->thd', grad_scores, key_g, preferred_element_type=jnp....  7.76 us
  transfers between devices with their start and end apart: 14, of which 8 were waited for; matrix products, arithmetic and copies ran while one was open for 5% of the time, Pallas kernels for 0%

profile of v1, /device:TPU:0, one launch (start us, length us, event | category | flops | bytes accessed | tf_op | source)
XLA Modules:
  0.0 265.7 jit_solution(13422360659507364431)
XLA Ops:
  7.2 1.2 copy.69
  8.4 2.4 collective-permute-start.3
  10.8 1.1 copy.66
  11.9 4.6 %collective-permute-start = (bf16[256,512]{0,1:T(8,128)(2,1)S(1)}, bf16[256,512]{0,1:T(8,128)(2,1)S(1)}, u32[]{:S(2)}, u32[]{:S(2)}) collective-permute-start(bf16[256,512]{0,1:T(8,128)(2,1)S(1)} %bitcast.190), channel_id=1, source_target_pairs={{0,1},{1,4},{4,5},{5,8},{8,9},{9,12},{12,13},{2,3},{3,6},{6,7},{7,... | collective-permute-start | bytes 786440 | tf_op jit(solution)/shard_map/ppermute | solution.py:18
  16.5 2.9 %collective-permute-start.4 = (bf16[256,512]{0,1:T(8,128)(2,1)S(1)}, bf16[256,512]{0,1:T(8,128)(2,1)}, u32[]{:S(2)}, u32[]{:S(2)}) collective-permute-start(bf16[256,512]{0,1:T(8,128)(2,1)S(1)} %collective-permute-done.3), channel_id=1, source_target_pairs={{0,1},{1,4},{4,5},{5,8},{8,9},{9,12},{12,13},{2,3},{3,6},{6,7},{7,... | collective-permute-start | bytes 786440 | tf_op jit(solution)/shard_map/ppermute | solution.py:18
  19.4 3.7 %collective-permute-start.1 = (bf16[256,512]{0,1:T(8,128)(2,1)S(1)}, bf16[256,512]{0,1:T(8,128)(2,1)S(1)}, u32[]{:S(2)}, u32[]{:S(2)}) collective-permute-start(bf16[256,512]{0,1:T(8,128)(2,1)S(1)} %collective-permute-done), channel_id=1, source_target_pairs={{0,1},{1,4},{4,5},{5,8},{8,9},{9,12},{12,13},{2,3},{3,6},{6,7},{7,... | collective-permute-start | bytes 786440 | tf_op jit(solution)/shard_map/ppermute | solution.py:18
  23.9 3.7 %collective-permute-start.5 = (bf16[256,512]{0,1:T(8,128)(2,1)}, bf16[256,512]{0,1:T(8,128)(2,1)}, u32[]{:S(2)}, u32[]{:S(2)}) collective-permute-start(bf16[256,512]{0,1:T(8,128)(2,1)} %collective-permute-done.4), channel_id=1, source_target_pairs={{0,1},{1,4},{4,5},{5,8},{8,9},{9,12},{12,13},{2,3},{3,6},{6,7},{7,... | collective-permute-start | bytes 786440 | tf_op jit(solution)/shard_map/ppermute | solution.py:18
  27.6 4.0 %collective-permute-start.2 = (bf16[256,512]{0,1:T(8,128)(2,1)S(1)}, bf16[256,512]{0,1:T(8,128)(2,1)}, u32[]{:S(2)}, u32[]{:S(2)}) collective-permute-start(bf16[256,512]{0,1:T(8,128)(2,1)S(1)} %collective-permute-done.1), channel_id=1, source_target_pairs={{0,1},{1,4},{4,5},{5,8},{8,9},{9,12},{12,13},{2,3},{3,6},{6,7},{7,... | collective-permute-start | bytes 786440 | tf_op jit(solution)/shard_map/ppermute | solution.py:18
  31.6 1.2 copy.68
  32.9 1.0 copy.71
  33.9 2.1 pad_maximum_fusion.1
  36.0 1.1 pad_maximum_fusion
  37.1 35.7 %while.15 = (s32[]{:T(128)}, bf16[2,256,2,256]{1,3,2,0:T(8,128)(2,1)}, f32[2,1024,256]{2,1,0:T(8,128)}, f32[2,1024,256]{2,1,0:T(8,128)}, s32[2]{0:T(128)S(1)}, /...) while((s32[]{:T(128)}, ...), condition=%wide.region_5.6_spmd.clone, body=%wide.region_1.5_spmd.clone.sunk | while | flops 1353977856 | bytes 41701704 | solution.py:59
  40.1 2.4 fusion.90
  42.4 1.6 fusion.89
  44.0 3.9 %fusion.91 = bf16[2,256,2,256]{1,3,2,0:T(8,128)(2,1)} fusion(bf16[2,256,2,256]{1,3,2,0:T(8,128)(2,1)} %get-tuple-element.259, s32[]{:T(128)S(6)} %copy.112, f32[1024,256,2]{1,0,2:T(8,128)S(1)} %fusion.89, bf16[1024,2,256]{0,2,1:T(8,128)(2,1)} %copy-done.3, s32[]{:T(128)S(6)} %select_n.34, f32[2,256,1024]{1,2,0:T(8,128)} %get-tuple-element.241, ...), kind=kOutput, calls=%fused_computation.16.clone.1 | convolution fusion | flops 272107008 | bytes 9441288 | tf_op jit(solution)/shard_map/while/body/eval_jaxpr/htk,kd->thd/dot_general | solution.py:54
  47.9 3.9 %fusion.92 = f32[2,1024,256]{2,1,0:T(8,128)} fusion(f32[2,1024,256]{2,1,0:T(8,128)} %get-tuple-element.260, s32[]{:T(128)S(6)} %copy.112, f32[1024,256,2]{1,0,2:T(8,128)S(1)} %fusion.89, bf16[256,2,2,256]{0,3,2,1:T(8,128)(2,1)} %copy-done.8, s32[]{:T(128)S(6)} %select_n.34, f32[2,256,1024]{1,2,0:T(8,128)} %get-tuple-element.241, ...), kind=kOutput, calls=%fused_computation.14.clone.1 | convolution fusion | flops 272107008 | bytes 9703432 | tf_op jit(solution)/shard_map/while/body/eval_jaxpr/htk,thd->kd/dot_general | solution.py:55
  51.8 3.2 %fusion.93 = f32[2,1024,256]{2,1,0:T(8,128)} fusion(f32[2,1024,256]{2,1,0:T(8,128)} %get-tuple-element.261, s32[]{:T(128)S(6)} %copy.112, bf16[256,2,2,256]{0,3,2,1:T(8,128)(2,1)} %get-tuple-element.281, s32[]{:T(128)S(6)} %select_n.34, f32[2,256,1024]{1,2,0:T(8,128)} %get-tuple-element.241, f32[2,256]{1,0:T(2,128)S(1)} %get-tuple-element.242), kind=kOutput, calls=%fused_computation.12.clone.1 | convolution fusion | flops 269484032 | bytes 3409928 | tf_op jit(solution)/shard_map/while/body/eval_jaxpr/htk,thd->kd/dot_general | solution.py:56
  57.9 2.4 fusion.90
  60.3 1.6 fusion.89
  61.9 3.9 %fusion.91 = bf16[2,256,2,256]{1,3,2,0:T(8,128)(2,1)} fusion(bf16[2,256,2,256]{1,3,2,0:T(8,128)(2,1)} %get-tuple-element.259, s32[]{:T(128)S(6)} %copy.112, f32[1024,256,2]{1,0,2:T(8,128)S(1)} %fusion.89, bf16[1024,2,256]{0,2,1:T(8,128)(2,1)} %copy-done.3, s32[]{:T(128)S(6)} %select_n.34, f32[2,256,1024]{1,2,0:T(8,128)} %get-tuple-element.241, ...), kind=kOutput, calls=%fused_computation.16.clone.1 | convolution fusion | flops 272107008 | bytes 9441288 | tf_op jit(solution)/shard_map/while/body/eval_jaxpr/htk,kd->thd/dot_general | solution.py:54
  65.7 3.9 %fusion.92 = f32[2,1024,256]{2,1,0:T(8,128)} fusion(f32[2,1024,256]{2,1,0:T(8,128)} %get-tuple-element.260, s32[]{:T(128)S(6)} %copy.112, f32[1024,256,2]{1,0,2:T(8,128)S(1)} %fusion.89, bf16[256,2,2,256]{0,3,2,1:T(8,128)(2,1)} %copy-done.8, s32[]{:T(128)S(6)} %select_n.34, f32[2,256,1024]{1,2,0:T(8,128)} %get-tuple-element.241, ...), kind=kOutput, calls=%fused_computation.14.clone.1 | convolution fusion | flops 272107008 | bytes 9703432 | tf_op jit(solution)/shard_map/while/body/eval_jaxpr/htk,thd->kd/dot_general | solution.py:55
  69.7 3.1 %fusion.93 = f32[2,1024,256]{2,1,0:T(8,128)} fusion(f32[2,1024,256]{2,1,0:T(8,128)} %get-tuple-element.261, s32[]{:T(128)S(6)} %copy.112, bf16[256,2,2,256]{0,3,2,1:T(8,128)(2,1)} %get-tuple-element.281, s32[]{:T(128)S(6)} %select_n.34, f32[2,256,1024]{1,2,0:T(8,128)} %get-tuple-element.241, f32[2,256]{1,0:T(2,128)S(1)} %get-tuple-element.242), kind=kOutput, calls=%fused_computation.12.clone.1 | convolution fusion | flops 269484032 | bytes 3409928 | tf_op jit(solution)/shard_map/while/body/eval_jaxpr/htk,thd->kd/dot_general | solution.py:56
  72.8 1.1 fusion.61
  73.9 1.3 collective-permute-start.9
  75.2 1.5 slice_bitcast_fusion.2
  77.5 1.3 collective-permute-start.10
  78.8 6.1 %collective-permute-done.10 = bf16[256,512]{1,0:T(8,128)(2,1)S(1)} collective-permute-done((bf16[256,512]{1,0:T(8,128)(2,1)S(1)}, bf16[256,512]{1,0:T(8,128)(2,1)S(1)}, u32[]{:S(2)}, u32[]{:S(2)}) %collective-permute-start.10) | collective-permute-done | bytes 262176 | tf_op jit(solution)/shard_map/ppermute | solution.py:18
  85.0 1.3 collective-permute-start.11
  86.4 6.3 %collective-permute-done.11 = bf16[256,512]{1,0:T(8,128)(2,1)S(1)} collective-permute-done((bf16[256,512]{1,0:T(8,128)(2,1)S(1)}, bf16[256,512]{1,0:T(8,128)(2,1)S(1)}, u32[]{:S(2)}, u32[]{:S(2)}) %collective-permute-start.11) | collective-permute-done | bytes 262176 | tf_op jit(solution)/shard_map/ppermute | solution.py:18
  93.4 0.8 fusion.57
  94.3 2.4 copy.90
  96.8 39.5 %reduce-scatter.4.cloned.1.call-done = bf16[1152,512]{1,0:T(8,128)(2,1)} async-done(((bf16[2304,512]{1,0:T(8,128)(2,1)}), bf16[1152,512]{1,0:T(8,128)(2,1)}) %reduce-scatter.4.cloned.1.call-update) | async-done | bytes 1179664
  136.3 2.4 copy.91
  138.7 1.1 fusion.60
  139.8 1.3 collective-permute-start.6
  141.1 1.5 slice_bitcast_fusion.5
  143.3 1.3 collective-permute-start.7
  144.6 5.9 %collective-permute-done.7 = bf16[256,512]{1,0:T(8,128)(2,1)S(1)} collective-permute-done((bf16[256,512]{1,0:T(8,128)(2,1)S(1)}, bf16[256,512]{1,0:T(8,128)(2,1)S(1)}, u32[]{:S(2)}, u32[]{:S(2)}) %collective-permute-start.7) | collective-permute-done | bytes 262176 | tf_op jit(solution)/shard_map/ppermute | solution.py:18
  150.6 1.5 collective-permute-start.8
  152.1 1.0 copy.88
  154.0 14.2 %collective-permute-done.8 = bf16[256,512]{1,0:T(8,128)(2,1)S(1)} collective-permute-done((bf16[256,512]{1,0:T(8,128)(2,1)S(1)}, bf16[256,512]{1,0:T(8,128)(2,1)S(1)}, u32[]{:S(2)}, u32[]{:S(2)}) %collective-permute-start.8) | collective-permute-done | bytes 262176 | tf_op jit(solution)/shard_map/ppermute | solution.py:18
  168.2 0.8 fusion.59
  169.0 65.9 %all-gather.3.cloned.1.call-done = bf16[9216,512]{0,1:T(8,128)(2,1)} async-done(((bf16[1152,512]{0,1:T(8,128)(2,1)}), bf16[9216,512]{0,1:T(8,128)(2,1)}) %all-gather.3.cloned.1.call-update) | async-done | bytes 9437200 | tf_op jit(solution)/shard_map/all_gather | solution.py:11
  234.9 9.5 %copy.104 = bf16[64,8,8,1152]{3,2,1,0:T(8,128)(2,1)} copy(bf16[64,8,8,1152]{3,1,2,0:T(8,128)(2,1)} %bitcast.177) | data formatting | bytes 18874368
  244.4 11.0 %bitcast_reduce_fusion = bf16[1152,512]{0,1:T(8,128)(2,1)} fusion(bf16[64,8,8,1152]{3,2,1,0:T(8,128)(2,1)} %copy.104), kind=kLoop, calls=%fused_computation.52 | loop fusion | flops 4128768 | bytes 10616832 | tf_op jit(solution)/shard_map/reduce_sum | solution.py:12
  255.4 1.4 convert_multiply_fusion
  256.9 2.0 copy.85
  (67 shorter events, 6.2 us)
Async XLA Ops:
  7.2 86.3 %copy-start = (bf16[1,256,2304]{2,1,0:T(8,128)(2,1)S(1)}, bf16[1,256,2304]{2,1,0:T(8,128)(2,1)}, u32[]{:S(2)}) copy-start(bf16[1,256,2304]{2,1,0:T(8,128)(2,1)} %param.8) | copy-start | bytes 3538948
  7.2 25.7 %copy-start.7 = (bf16[1,256,1024]{2,1,0:T(8,128)(2,1)S(1)}, bf16[1,256,1024]{2,1,0:T(8,128)(2,1)}, u32[]{:S(2)}) copy-start(bf16[1,256,1024]{2,1,0:T(8,128)(2,1)} %param.12) | copy-start | bytes 1572868
  7.2 129.1 %reduce-scatter.4.cloned.1.call-start = ((), (), s32[]{:S(2)}) async-start(), calls=%async_computation.2 | async-start | bytes 3538944
  8.4 8.1 %collective-permute-start.3 = (bf16[256,512]{0,1:T(8,128)(2,1)S(1)}, bf16[256,512]{0,1:T(8,128)(2,1)S(1)}, u32[]{:S(2)}, u32[]{:S(2)}) collective-permute-start(bf16[256,512]{0,1:T(8,128)(2,1)S(1)} %bitcast.192), channel_id=1, source_target_pairs={{0,1},{1,4},{4,5},{5,8},{8,9},{9,12},{12,13},{2,3},{3,6},{6,7},{7,... | collective-permute-start | bytes 786440 | tf_op jit(solution)/shard_map/ppermute | solution.py:18
  11.9 7.5 %collective-permute-start = (bf16[256,512]{0,1:T(8,128)(2,1)S(1)}, bf16[256,512]{0,1:T(8,128)(2,1)S(1)}, u32[]{:S(2)}, u32[]{:S(2)}) collective-permute-start(bf16[256,512]{0,1:T(8,128)(2,1)S(1)} %bitcast.190), channel_id=1, source_target_pairs={{0,1},{1,4},{4,5},{5,8},{8,9},{9,12},{12,13},{2,3},{3,6},{6,7},{7,... | collective-permute-start | bytes 786440 | tf_op jit(solution)/shard_map/ppermute | solution.py:18
  16.5 7.4 %collective-permute-start.4 = (bf16[256,512]{0,1:T(8,128)(2,1)S(1)}, bf16[256,512]{0,1:T(8,128)(2,1)}, u32[]{:S(2)}, u32[]{:S(2)}) collective-permute-start(bf16[256,512]{0,1:T(8,128)(2,1)S(1)} %collective-permute-done.3), channel_id=1, source_target_pairs={{0,1},{1,4},{4,5},{5,8},{8,9},{9,12},{12,13},{2,3},{3,6},{6,7},{7,... | collective-permute-start | bytes 786440 | tf_op jit(solution)/shard_map/ppermute | solution.py:18
  19.4 8.2 %collective-permute-start.1 = (bf16[256,512]{0,1:T(8,128)(2,1)S(1)}, bf16[256,512]{0,1:T(8,128)(2,1)S(1)}, u32[]{:S(2)}, u32[]{:S(2)}) collective-permute-start(bf16[256,512]{0,1:T(8,128)(2,1)S(1)} %collective-permute-done), channel_id=1, source_target_pairs={{0,1},{1,4},{4,5},{5,8},{8,9},{9,12},{12,13},{2,3},{3,6},{6,7},{7,... | collective-permute-start | bytes 786440 | tf_op jit(solution)/shard_map/ppermute | solution.py:18
  23.9 10.0 %collective-permute-start.5 = (bf16[256,512]{0,1:T(8,128)(2,1)}, bf16[256,512]{0,1:T(8,128)(2,1)}, u32[]{:S(2)}, u32[]{:S(2)}) collective-permute-start(bf16[256,512]{0,1:T(8,128)(2,1)} %collective-permute-done.4), channel_id=1, source_target_pairs={{0,1},{1,4},{4,5},{5,8},{8,9},{9,12},{12,13},{2,3},{3,6},{6,7},{7,... | collective-permute-start | bytes 786440 | tf_op jit(solution)/shard_map/ppermute | solution.py:18
  27.6 8.4 %collective-permute-start.2 = (bf16[256,512]{0,1:T(8,128)(2,1)S(1)}, bf16[256,512]{0,1:T(8,128)(2,1)}, u32[]{:S(2)}, u32[]{:S(2)}) collective-permute-start(bf16[256,512]{0,1:T(8,128)(2,1)S(1)} %collective-permute-done.1), channel_id=1, source_target_pairs={{0,1},{1,4},{4,5},{5,8},{8,9},{9,12},{12,13},{2,3},{3,6},{6,7},{7,... | collective-permute-start | bytes 786440 | tf_op jit(solution)/shard_map/ppermute | solution.py:18
  37.1 5.3 %copy-start.3 = (bf16[1024,2,256]{0,2,1:T(8,128)(2,1)}, bf16[1024,2,256]{0,2,1:T(8,128)(2,1)S(1)}, u32[]{:S(2)}) copy-start(bf16[1024,2,256]{0,2,1:T(8,128)(2,1)S(1)} %get-tuple-element.278) | copy-start | bytes 3145732 | tf_op jit(solution)/shard_map/while
  37.1 5.3 %copy-start.8 = (bf16[256,2,2,256]{0,3,2,1:T(8,128)(2,1)}, bf16[256,2,2,256]{0,3,2,1:T(8,128)(2,1)S(1)}, u32[]{:S(2)}) copy-start(bf16[256,2,2,256]{0,3,2,1:T(8,128)(2,1)S(1)} %get-tuple-element.279) | copy-start | bytes 1572868 | tf_op jit(solution)/shard_map/while
  51.8 3.2 %copy-start.4 = (bf16[1024,2,256]{0,2,1:T(8,128)(2,1)S(1)}, bf16[1024,2,256]{0,2,1:T(8,128)(2,1)}, u32[]{:S(2)}) copy-start(bf16[1024,2,256]{0,2,1:T(8,128)(2,1)} %copy-done.3) | copy-start | bytes 3145732 | tf_op jit(solution)/shard_map/while
  51.8 3.2 %copy-start.9 = (bf16[256,2,2,256]{0,3,2,1:T(8,128)(2,1)S(1)}, bf16[256,2,2,256]{0,3,2,1:T(8,128)(2,1)}, u32[]{:S(2)}) copy-start(bf16[256,2,2,256]{0,3,2,1:T(8,128)(2,1)} %copy-done.8) | copy-start | bytes 1572868 | tf_op jit(solution)/shard_map/while
  55.0 5.3 %copy-start.3 = (bf16[1024,2,256]{0,2,1:T(8,128)(2,1)}, bf16[1024,2,256]{0,2,1:T(8,128)(2,1)S(1)}, u32[]{:S(2)}) copy-start(bf16[1024,2,256]{0,2,1:T(8,128)(2,1)S(1)} %get-tuple-element.278) | copy-start | bytes 3145732 | tf_op jit(solution)/shard_map/while
  55.0 5.3 %copy-start.8 = (bf16[256,2,2,256]{0,3,2,1:T(8,128)(2,1)}, bf16[256,2,2,256]{0,3,2,1:T(8,128)(2,1)S(1)}, u32[]{:S(2)}) copy-start(bf16[256,2,2,256]{0,3,2,1:T(8,128)(2,1)S(1)} %get-tuple-element.279) | copy-start | bytes 1572868 | tf_op jit(solution)/shard_map/while
  69.7 3.2 %copy-start.4 = (bf16[1024,2,256]{0,2,1:T(8,128)(2,1)S(1)}, bf16[1024,2,256]{0,2,1:T(8,128)(2,1)}, u32[]{:S(2)}) copy-start(bf16[1024,2,256]{0,2,1:T(8,128)(2,1)} %copy-done.3) | copy-start | bytes 3145732 | tf_op jit(solution)/shard_map/while
  69.7 3.2 %copy-start.9 = (bf16[256,2,2,256]{0,3,2,1:T(8,128)(2,1)S(1)}, bf16[256,2,2,256]{0,3,2,1:T(8,128)(2,1)}, u32[]{:S(2)}) copy-start(bf16[256,2,2,256]{0,3,2,1:T(8,128)(2,1)} %copy-done.8) | copy-start | bytes 1572868 | tf_op jit(solution)/shard_map/while
  73.9 3.4 %collective-permute-start.9 = (bf16[256,512]{1,0:T(8,128)(2,1)S(1)}, bf16[256,512]{1,0:T(8,128)(2,1)S(1)}, u32[]{:S(2)}, u32[]{:S(2)}) collective-permute-start(bf16[256,512]{1,0:T(8,128)(2,1)S(1)} %bitcast.196), channel_id=1, source_target_pairs={{1,0},{4,1},{5,4},{8,5},{9,8},{12,9},{13,12},{3,2},{6,3},{7,6},{10... | collective-permute-start | bytes 786440 | tf_op jit(solution)/shard_map/ppermute | solution.py:18
  77.5 7.5 %collective-permute-start.10 = (bf16[256,512]{1,0:T(8,128)(2,1)S(1)}, bf16[256,512]{1,0:T(8,128)(2,1)S(1)}, u32[]{:S(2)}, u32[]{:S(2)}) collective-permute-start(bf16[256,512]{1,0:T(8,128)(2,1)S(1)} %add_convert_fusion.2), channel_id=1, source_target_pairs={{1,0},{4,1},{5,4},{8,5},{9,8},{12,9},{13,12},{3,2},{6,3},{7,6},{10... | collective-permute-start | bytes 786440 | tf_op jit(solution)/shard_map/ppermute | solution.py:18
  85.0 7.7 %collective-permute-start.11 = (bf16[256,512]{1,0:T(8,128)(2,1)S(1)}, bf16[256,512]{1,0:T(8,128)(2,1)S(1)}, u32[]{:S(2)}, u32[]{:S(2)}) collective-permute-start(bf16[256,512]{1,0:T(8,128)(2,1)S(1)} %add_convert_fusion.1), channel_id=1, source_target_pairs={{1,0},{4,1},{5,4},{8,5},{9,8},{12,9},{13,12},{3,2},{6,3},{7,6},{10... | collective-permute-start | bytes 786440 | tf_op jit(solution)/shard_map/ppermute | solution.py:18
  86.4 6.3 %copy-start.1 = (f32[2,32,8,256]{3,2,0,1:T(8,128)}, f32[2,32,8,256]{3,2,0,1:T(8,128)S(1)}, u32[]{:S(2)}) copy-start(f32[2,32,8,256]{3,2,0,1:T(8,128)S(1)} %copy.103) | copy-start | bytes 1572868
  92.7 0.7 copy-start.5
  96.7 138.2 %all-gather.3.cloned.1.call-start = ((), (), s32[]{:S(2)}) async-start(), calls=%async_computation.1 | async-start | bytes 10616832 | tf_op jit(solution)/shard_map/all_gather | solution.py:11
  139.8 3.4 %collective-permute-start.6 = (bf16[256,512]{1,0:T(8,128)(2,1)S(1)}, bf16[256,512]{1,0:T(8,128)(2,1)S(1)}, u32[]{:S(2)}, u32[]{:S(2)}) collective-permute-start(bf16[256,512]{1,0:T(8,128)(2,1)S(1)} %bitcast.197), channel_id=1, source_target_pairs={{1,0},{4,1},{5,4},{8,5},{9,8},{12,9},{13,12},{3,2},{6,3},{7,6},{10... | collective-permute-start | bytes 786440 | tf_op jit(solution)/shard_map/ppermute | solution.py:18
  142.5 9.6 %copy-start.10 = (bf16[2,256,2,256]{1,3,2,0:T(8,128)(2,1)S(1)}, bf16[2,256,2,256]{1,3,2,0:T(8,128)(2,1)}, u32[]{:S(2)}) copy-start(bf16[2,256,2,256]{1,3,2,0:T(8,128)(2,1)} %get-tuple-element.58) | copy-start | bytes 1572868
  143.3 7.3 %collective-permute-start.7 = (bf16[256,512]{1,0:T(8,128)(2,1)S(1)}, bf16[256,512]{1,0:T(8,128)(2,1)S(1)}, u32[]{:S(2)}, u32[]{:S(2)}) collective-permute-start(bf16[256,512]{1,0:T(8,128)(2,1)S(1)} %add_convert_fusion.5), channel_id=1, source_target_pairs={{1,0},{4,1},{5,4},{8,5},{9,8},{12,9},{13,12},{3,2},{6,3},{7,6},{10... | collective-permute-start | bytes 786440 | tf_op jit(solution)/shard_map/ppermute | solution.py:18
  144.6 8.6 %copy-start.2 = (f32[2,32,8,256]{3,2,0,1:T(8,128)S(1)}, f32[2,32,8,256]{3,2,0,1:T(8,128)}, u32[]{:S(2)}) copy-start(f32[2,32,8,256]{3,2,0,1:T(8,128)} %copy-done.1) | copy-start | bytes 1572868
  144.6 8.6 %copy-start.6 = (bf16[256,512]{1,0:T(8,128)(2,1)S(1)}, bf16[256,512]{1,0:T(8,128)(2,1)}, u32[]{:S(2)}) copy-start(bf16[256,512]{1,0:T(8,128)(2,1)} %copy-done.5) | copy-start | bytes 786436
  150.6 17.6 %collective-permute-start.8 = (bf16[256,512]{1,0:T(8,128)(2,1)S(1)}, bf16[256,512]{1,0:T(8,128)(2,1)S(1)}, u32[]{:S(2)}, u32[]{:S(2)}) collective-permute-start(bf16[256,512]{1,0:T(8,128)(2,1)S(1)} %add_convert_fusion.4), channel_id=1, source_target_pairs={{1,0},{4,1},{5,4},{8,5},{9,8},{12,9},{13,12},{3,2},{6,3},{7,6},{10... | collective-permute-start | bytes 786440 | tf_op jit(solution)/shard_map/ppermute | solution.py:18
Sparse Core Ops, SparseCore 0:
  96.9 39.3 reduce-scatter.3
  138.8 96.1 all-gather.2
